TPU v7x, 32 devices: a whole 2x2x4 slice. The times are simulated.
32 devices in a mesh: group: 2 (over x), node: 16 (over z, y, core).
Axes of the slice: x: 2, y: 2, z: 4, core: 2. Of those that a mesh axis runs over, the one named last changes fastest.
Arguments:
- states: bfloat16 [512, 2048], P(('group', 'node')), parts along dimension 0, may hold values from -400 to 400
- norm_gain: float32 [2048], replicated, may hold values from 0.5 to 1.5
- picks: int32 [512, 8], P(('group', 'node')), parts along dimension 0, may hold values from 0 to 15, all different within a row; in each aligned block of 16 rows (0 to 15, 16 to 31, ...) at most 16 rows name the same one
- gate_weights: float32 [512, 8], P(('group', 'node')), parts along dimension 0, may hold values from 0.05 to 1
- w_gate: bfloat16 [16, 2048, 768], P('node'), may hold values from -0.125 to 0.125
- w_up: bfloat16 [16, 2048, 768], P('node'), may hold values from -0.125 to 0.125
- w_down: bfloat16 [16, 768, 2048], P('node'), may hold values from -0.21875 to 0.21875
- queries: bfloat16 [128, 4096], P(('group', 'node')), parts along dimension 0, may hold values from -88 to 88
- keys: bfloat16 [128, 256, 512], P(('group', 'node')), parts along dimension 0, may hold values from -4 to 4
- values: bfloat16 [128, 256, 512], P(('group', 'node')), parts along dimension 0, may hold values from -4 to 4
- incoming_keys: bfloat16 [128, 512], P(('group', 'node')), parts along dimension 0, may hold values from -4 to 4
- incoming_values: bfloat16 [128, 512], P(('group', 'node')), parts along dimension 0, may hold values from -4 to 4
- lengths: int32 [128], P(('group', 'node')), parts along dimension 0, may hold values from 32 to 256, as said below
Outputs:
- moe_output: bfloat16 [512, 2048], P(('group', 'node')), parts along dimension 0
- attention_output: bfloat16 [128, 4096], P(('group', 'node')), parts along dimension 0
There are 2 independent parts, one for each index of `group`. A program takes and returns all parts, laid end to end along the dimension named above; an argument that names none is the same for every part. Nothing has to cross between parts.
Inputs may be any that keep to these rules, and one draw needn't show every extreme that they name: Each token picks 8 different experts; among the 16 tokens of one device no expert is picked by more than 16 tokens, a bound that some block reaches. `lengths`: the first request of each device holds 256 cached tokens.
All inputs are finite; a program needn't handle non-finite values.
Results may differ from a plain program's by a relative error of at most 0.0085.
Values may be sent and summed in bfloat16 or wider, within the bound.
No kernel may reach another device: no remote copies, remote signals or barrier semaphores. Data moves between devices by JAX's collectives and lax.ppermute only.
A program may use at most 64 MiB of HBM per device.

v0:
```python
import math
import jax
import jax.numpy as jnp
from jax import lax
from jax.sharding import PartitionSpec as P

QUERY_HEADS = 32
KEY_VALUE_HEADS = 4
HEAD_WIDTH = 128
TOPK = 8
TOK_DEV = 16


def expert_block(received, w_gate, w_up, w_down):
    peers = lax.axis_size("node")
    local_experts = w_gate.shape[0]
    slot_count = received.shape[1]
    features = received.shape[2]
    grouped = received.reshape(peers, local_experts, slot_count, features)
    gate_part = jnp.einsum("nesd,edf->nesf", grouped, w_gate, preferred_element_type=jnp.float32)
    up_part = jnp.einsum("nesd,edf->nesf", grouped, w_up, preferred_element_type=jnp.float32)
    inner = (jax.nn.silu(gate_part) * up_part).astype(jnp.bfloat16)
    produced = jnp.einsum(
        "nesf,efd->nesd", inner, w_down, preferred_element_type=jnp.float32
    ).astype(jnp.bfloat16)
    return produced.reshape(peers * local_experts, slot_count, features)


def route_block(normed, picks, gate_weights, w_gate, w_up, w_down, capacity):
    rows_here = picks.shape[0]
    picks_here = picks.shape[1]
    experts_all = w_gate.shape[0] * lax.axis_size("node")
    features = normed.shape[1]
    flattened = picks.reshape(-1)
    expert_ids = jnp.arange(experts_all, dtype=jnp.int32)
    onehot = (flattened[:, None] == expert_ids[None, :]).astype(jnp.int32)
    earlier = jnp.cumsum(onehot, axis=0) - onehot
    slot_of = jnp.sum(earlier * onehot, axis=1)
    target = flattened * capacity + slot_of
    layout = jnp.arange(experts_all * capacity, dtype=jnp.int32)
    placed = jnp.sum(
        (layout[:, None, None] == target.reshape(rows_here, picks_here)[None, :, :]).astype(
            jnp.int32
        ),
        axis=2,
    )
    outgoing = jnp.dot(placed.astype(jnp.bfloat16), normed, preferred_element_type=jnp.float32)
    outgoing = outgoing.astype(jnp.bfloat16).reshape(experts_all, capacity, features)
    produced = expert_block(
        lax.all_to_all(outgoing, "node", split_axis=0, concat_axis=0, tiled=True),
        w_gate,
        w_up,
        w_down,
    )
    returned = lax.all_to_all(produced, "node", split_axis=0, concat_axis=0, tiled=True)
    gathered = jnp.take(returned.reshape(experts_all * capacity, features), target, axis=0)
    gathered = gathered.reshape(rows_here, picks_here, features)
    shares = gate_weights / jnp.sum(gate_weights, axis=1, keepdims=True)
    return jnp.einsum("tk,tkd->td", shares, gathered.astype(jnp.float32)).astype(jnp.bfloat16)


def dense_block(normed, picks, gate_weights, w_gate, w_up, w_down):
    local_experts = w_gate.shape[0]
    node_index = lax.axis_index("node")
    experts_all = local_experts * lax.axis_size("node")
    shares = gate_weights / jnp.sum(gate_weights, axis=1, keepdims=True)
    expert_ids = jnp.arange(experts_all, dtype=jnp.int32)
    chosen = picks[:, :, None] == expert_ids[None, None, :]
    dense_shares = jnp.sum(jnp.where(chosen, shares[:, :, None], 0.0), axis=1)
    every_row = lax.all_gather(normed, "node", axis=0, tiled=True)
    every_share = lax.all_gather(dense_shares, "node", axis=0, tiled=True)
    own_shares = lax.dynamic_slice_in_dim(
        every_share, node_index * local_experts, local_experts, axis=1
    )
    summed = None
    for expert in range(local_experts):
        gate_part = jnp.dot(every_row, w_gate[expert], preferred_element_type=jnp.float32)
        up_part = jnp.dot(every_row, w_up[expert], preferred_element_type=jnp.float32)
        inner = (jax.nn.silu(gate_part) * up_part).astype(jnp.bfloat16)
        produced = jnp.dot(inner, w_down[expert], preferred_element_type=jnp.float32).astype(
            jnp.bfloat16
        )
        column = own_shares[:, expert : expert + 1]
        weighted = jnp.where(column != 0.0, column * produced.astype(jnp.float32), 0.0)
        summed = weighted if summed is None else summed + weighted
    total = lax.psum_scatter(summed, "node", scatter_dimension=0, tiled=True)
    return total.astype(jnp.bfloat16)


def attend(queries, keys, values, incoming_keys, incoming_values, lengths):
    request_rows = queries.shape[0]
    valid_length = keys.shape[1]
    query_groups = QUERY_HEADS // KEY_VALUE_HEADS
    score_scale = 1.0 / math.sqrt(HEAD_WIDTH)
    query_rows = queries.reshape(request_rows, KEY_VALUE_HEADS, query_groups, HEAD_WIDTH)
    stored_keys = keys.reshape(request_rows, valid_length, KEY_VALUE_HEADS, HEAD_WIDTH)
    stored_values = values.reshape(request_rows, valid_length, KEY_VALUE_HEADS, HEAD_WIDTH)
    scores = (
        jnp.einsum("rkgd,rlkd->rkgl", query_rows, stored_keys, preferred_element_type=jnp.float32)
        * score_scale
    )
    new_token_scores = (
        jnp.einsum(
            "behw,bew->beh",
            query_rows,
            incoming_keys.reshape(request_rows, KEY_VALUE_HEADS, HEAD_WIDTH),
            preferred_element_type=jnp.float32,
        )
        * score_scale
    )
    present = (jnp.arange(valid_length, dtype=jnp.int32)[None, :] < lengths[:, None])[
        :, None, None, :
    ]
    masked = jnp.where(present, scores, -1e30)
    highest = jnp.maximum(jnp.max(masked, axis=3), new_token_scores)
    raised = jnp.where(present, jnp.exp(masked - highest[..., None]), 0.0)
    fresh_raised = jnp.exp(new_token_scores - highest)
    denominator = jnp.sum(raised, axis=3) + fresh_raised
    probs = (raised / denominator[..., None]).astype(jnp.bfloat16)
    new_token_probability = (fresh_raised / denominator).astype(jnp.bfloat16)
    blended_output = jnp.einsum(
        "rkgl,rlkd->rkgd", probs, stored_values, preferred_element_type=jnp.float32
    )
    blended_output = blended_output + new_token_probability.astype(jnp.float32)[
        ..., None
    ] * incoming_values.reshape(request_rows, KEY_VALUE_HEADS, 1, HEAD_WIDTH).astype(jnp.float32)
    return blended_output.reshape(request_rows, QUERY_HEADS * HEAD_WIDTH).astype(jnp.bfloat16)


def on_device(
    states,
    norm_gain,
    picks,
    gate_weights,
    w_gate,
    w_up,
    w_down,
    queries,
    keys,
    values,
    incoming_keys,
    incoming_values,
    lengths,
):
    widened = states.astype(jnp.float32)
    meansq = jnp.mean(widened * widened, axis=1, keepdims=True) + 1e-06
    normed = (widened / jnp.sqrt(meansq) * norm_gain[None, :]).astype(jnp.bfloat16)
    experts_all = w_gate.shape[0] * lax.axis_size("node")
    capacity = min(TOK_DEV, max(2, 2 * TOK_DEV * TOPK // experts_all))
    gathered_rows = normed.shape[0] * lax.axis_size("node")
    if gathered_rows <= experts_all * capacity:
        moe_output = dense_block(normed, picks, gate_weights, w_gate, w_up, w_down)
    else:
        moe_output = route_block(normed, picks, gate_weights, w_gate, w_up, w_down, capacity)
    attention_output = attend(queries, keys, values, incoming_keys, incoming_values, lengths)
    return (moe_output, attention_output)


def solution(mesh):
    in_specs = (
        P(("group", "node"), None),
        P(),
        P(("group", "node"), None),
        P(("group", "node"), None),
        P("node", None, None),
        P("node", None, None),
        P("node", None, None),
        P(("group", "node"), None),
        P(("group", "node"), None, None),
        P(("group", "node"), None, None),
        P(("group", "node"), None),
        P(("group", "node"), None),
        P(("group", "node")),
    )
    out_specs = (P(("group", "node"), None), P(("group", "node"), None))
    return jax.shard_map(
        on_device, mesh=mesh, in_specs=in_specs, out_specs=out_specs, check_vma=False
    )
```

profile of v0, /device:TPU:0, one launch (start us, length us, event | category | flops | bytes accessed | tf_op | source)
XLA Modules:
  0.0 130.5 jit_solution(14957401448452033666)
XLA Ops:
  7.2 0.0 copy-start
  7.2 0.0 all-gather.2.cloned.1.call-start
  7.2 1.1 fusion.38
  8.4 1.6 %fusion.40 = bf16[16,2048]{1,0:T(8,128)(2,1)} fusion(bf16[16,2048]{1,0:T(8,128)(2,1)} %param.13, f32[2048]{0:T(1024)} %param.14, f32[16]{0:T(128)S(1)} %add_sqrt_fusion), kind=kLoop, calls=%fused_computation.30 | loop fusion | flops 131072 | bytes 139328 | tf_op jit(solution)/shard_map/convert_element_type | solution.py:147
  9.9 0.0 all-gather.2.cloned.1.call-update
  9.9 0.0 reduce-scatter.2.cloned.1.call-start
  10.0 0.7 reduce_sum.36
  10.7 0.7 broadcast_divide_fusion
  11.4 0.1 copy.28
  11.5 0.8 copy.27
  12.2 0.1 select_reduce_fusion
  12.3 23.5 %all_gather.6 = f32[256,16]{1,0:T(8,128)S(1)} all-gather(f32[16,16]{1,0:T(8,128)S(1)} %select_reduce_fusion), channel_id=1, replica_groups=mesh['group'=2,'node'=16] {'node'}, dimensions={0}, use_global_device_ids=true | all-gather | bytes 17408 | tf_op jit(solution)/shard_map/all_gather | solution.py:71
  35.9 0.2 dynamic-slice_reduce_fusion
  36.0 0.2 compare_reduce_fusion
  36.2 15.2 %all-gather.2.cloned.1.call-done = bf16[256,2048]{1,0:T(8,128)(2,1)} async-done(((bf16[16,2048]{1,0:T(8,128)(2,1)}), bf16[256,2048]{1,0:T(8,128)(2,1)}) %all-gather.2.cloned.1.call-update) | async-done | bytes 1048592 | tf_op jit(solution)/shard_map/all_gather | solution.py:70
  51.5 4.1 %fusion.4 = f32[256,768]{1,0:T(8,128)} fusion(bf16[256,2048]{1,0:T(8,128)(2,1)} %all-gather.2.cloned.1.call-done, bf16[1,2048,768]{2,1,0:T(8,128)(2,1)} %param.17), kind=kOutput, calls=%fused_computation.4 | convolution fusion | flops 805306368 | bytes 4980736 | tf_op jit(solution)/shard_map/dot_general | solution.py:77
  55.5 0.0 copy-done
  55.5 0.0 copy-start.2
  55.5 0.0 copy-start.3
  55.5 0.0 copy-start.4
  55.5 0.0 copy-start.1
  55.6 5.9 %fusion.15 = f32[256,2048]{1,0:T(8,128)} fusion(bf16[1,768,2048]{2,1,0:T(8,128)(2,1)S(1)} %copy-done, f32[256]{0:T(256)S(1)} %dynamic-slice_reduce_fusion, pred[256]{0:T(512)(128)(4,1)S(1)} %compare_reduce_fusion, bf16[256,2048]{1,0:T(8,128)(2,1)} %all-gather.2.cloned.1.call-done, bf16[1,2048,768]{2,1,0:T(8,128)(2,1)} %param.18, f32[256,768]{1,0:T(8,128)} %fusion.4), kind=kOutput, calls=%fused_computation.9 | convolution fusion | flops 1613889536 | bytes 10224896 | tf_op jit(solution)/shard_map/dot_general | solution.py:80
  61.5 0.0 reduce-scatter.2.cloned.1.call-update
  61.5 0.0 copy-done.2
  61.5 0.0 copy-done.3
  61.5 0.0 copy-done.4
  61.5 0.1 iota_compare_fusion.1
  61.6 0.0 copy-done.1
  61.6 0.1 fusion.46
  61.8 1.7 %fusion.55 = (f32[4,4,8]{2,1,0:T(4,128)S(1)}, f32[4,4,8,256]{3,2,1,0:T(8,128)S(1)}) fusion(bf16[1,4,32,128]{3,1,2,0:T(4,128)(2,1)S(1)} %bitcast.60, pred[4,256]{1,0:T(4,128)(4,1)S(1)} %iota_compare_fusion.1, bf16[4,256,512]{2,1,0:T(8,128)(2,1)} %param.21), kind=kOutput, calls=%fused_computation.58 | convolution fusion | flops 8486784 | bytes 1213952 | tf_op jit(solution)/shard_map/rkgd,rlkd->rkgl/dot_general | solution.py:99
  63.5 0.2 fusion.41
  63.7 1.5 %fusion.26 = bf16[1,4,32,128]{3,2,1,0:T(8,128)(2,1)S(1)} fusion(f32[4,4,8,256]{3,2,1,0:T(8,128)S(1)} %get-tuple-element.5, f32[4,4,8]{2,1,0:T(4,128)S(1)} %get-tuple-element.3, f32[4,4,8]{2,1,0:T(4,128)S(1)} %multiply_maximum_fusion, pred[4,256]{1,0:T(4,128)(4,1)S(1)} %iota_compare_fusion.1, f32[4,4,128]{2,1,0:T(4,128)S(1)} %reshape.64, ...), kind=kOutput, calls=%fused_computation.16 | convolution fusion | flops 8568832 | bytes 1223168 | tf_op jit(solution)/shard_map/rkgl,rlkd->rkgd/dot_general | solution.py:121
  65.2 0.6 copy.58
  65.9 56.2 %reduce-scatter.2.cloned.1.call-done = f32[16,2048]{1,0:T(8,128)} async-done(((f32[256,2048]{1,0:T(8,128)}), f32[16,2048]{1,0:T(8,128)}) %reduce-scatter.2.cloned.1.call-update) | async-done | bytes 131088 | tf_op jit(solution)/shard_map/reduce_scatter | solution.py:86
  122.1 1.5 %convert_element_type.49 = bf16[16,2048]{1,0:T(8,128)(2,1)} convert(f32[16,2048]{1,0:T(8,128)} %reduce-scatter.2.cloned.1.call-done) | non-fusion elementwise | flops 32768 | bytes 196608 | tf_op jit(solution)/shard_map/convert_element_type | solution.py:87
  (5 shorter events, 0.1 us)
Async XLA Ops:
  7.2 48.4 %copy-start = (bf16[1,768,2048]{2,1,0:T(8,128)(2,1)S(1)}, bf16[1,768,2048]{2,1,0:T(8,128)(2,1)}, u32[]{:S(2)}) copy-start(bf16[1,768,2048]{2,1,0:T(8,128)(2,1)} %param.19) | copy-start | bytes 9437188
  7.2 44.3 %all-gather.2.cloned.1.call-start = ((), (), s32[]{:S(2)}) async-start(), calls=%async_computation.1 | async-start | bytes 1114112 | tf_op jit(solution)/shard_map/all_gather | solution.py:70
  9.9 112.1 %reduce-scatter.2.cloned.1.call-start = ((), (), s32[]{:S(2)}) async-start(), calls=%async_computation.2 | async-start | bytes 2228224 | tf_op jit(solution)/shard_map/reduce_scatter | solution.py:86
  55.5 6.0 %copy-start.2 = (bf16[4,512]{1,0:T(4,128)(2,1)S(1)}, bf16[4,512]{1,0:T(4,128)(2,1)}, u32[]{:S(2)}) copy-start(bf16[4,512]{1,0:T(4,128)(2,1)} %param.23) | copy-start | bytes 12292
  55.5 6.0 %copy-start.3 = (bf16[4,512]{1,0:T(4,128)(2,1)S(1)}, bf16[4,512]{1,0:T(4,128)(2,1)}, u32[]{:S(2)}) copy-start(bf16[4,512]{1,0:T(4,128)(2,1)} %param.24) | copy-start | bytes 12292
  55.5 6.0 %copy-start.4 = (s32[4]{0:T(128)S(1)}, s32[4]{0:T(128)}, u32[]{:S(2)}) copy-start(s32[4]{0:T(128)} %param.25) | copy-start | bytes 52
  55.5 6.1 %copy-start.1 = (bf16[4,4096]{1,0:T(4,128)(2,1)S(1)}, bf16[4,4096]{1,0:T(4,128)(2,1)}, u32[]{:S(2)}) copy-start(bf16[4,4096]{1,0:T(4,128)(2,1)} %param.20) | copy-start | bytes 98308
Sparse Core Ops, SparseCore 0:
  10.7 40.6 all-gather.1
  61.6 60.4 reduce-scatter.1
where the time goes:
time: 131 us; the launch traced here: 130 us
  waiting for transfers between devices  71.5 us (55%)
  blocking collectives  23.5 us (18%)
  between operations  14.1 us (11%)
  matrix products  13.3 us (10%)
  other arithmetic  6.23 us (5%)
  local copies, waits for them, and re-layouts  1.71 us (1%)
    reduce_scatter x1, waiting for transfers between devices, dense_block(): total = lax.psum_scatter(summed, 'node', scatter_dimension=0, tiled=True)  56.2 us
    all_gather x1, blocking collectives, dense_block(): every_share = lax.all_gather(dense_shares, 'node', axis=0, tiled=True)  23.5 us
    all_gather x1, waiting for transfers between devices, dense_block(): every_row = lax.all_gather(normed, 'node', axis=0, tiled=True)  15.2 us
    dot_general x1, matrix products, dense_block(): jnp.dot(inner, w_down[expert], preferred_element_type=jnp.float32)  5.91 us
    dot_general x1, matrix products, dense_block(): jnp.dot(every_row, w_gate[expert], preferred_element_type=jnp.float32)  4.07 us
  transfers between devices with their start and end apart: 2, of which 2 were waited for; matrix products, arithmetic and copies ran while one was open for 5% of the time, Pallas kernels for 0%

commit v1 on v0

--- a/solution.py
+++ b/solution.py
@@ -68,7 +68,24 @@
     chosen = picks[:, :, None] == expert_ids[None, None, :]
     dense_shares = jnp.sum(jnp.where(chosen, shares[:, :, None], 0.0), axis=1)
     every_row = lax.all_gather(normed, "node", axis=0, tiled=True)
-    every_share = lax.all_gather(dense_shares, "node", axis=0, tiled=True)
+    ways, here, step = (lax.axis_size("node"), lax.axis_index("node"), dense_shares.shape[0])
+    shape = [n * ways if d == 0 else n for d, n in enumerate(dense_shares.shape)]
+    every_share = lax.dynamic_update_slice_in_dim(
+        jnp.zeros(shape, dense_shares.dtype), dense_shares, here * step, axis=0
+    )
+    going_up = going_down = dense_shares
+    for far in range(1, ways // 2 + 1):
+        going_up = lax.ppermute(going_up, "node", [(d, (d + 1) % ways) for d in range(ways)])
+        every_share = lax.dynamic_update_slice_in_dim(
+            every_share, going_up, (here - far) % ways * step, axis=0
+        )
+        if 2 * far < ways:
+            going_down = lax.ppermute(
+                going_down, "node", [(d, (d - 1) % ways) for d in range(ways)]
+            )
+            every_share = lax.dynamic_update_slice_in_dim(
+                every_share, going_down, (here + far) % ways * step, axis=0
+            )
     own_shares = lax.dynamic_slice_in_dim(
         every_share, node_index * local_experts, local_experts, axis=1
     )

time: 131 us -> 140 us (1.069)
  starting transfers between devices: 0.08 us -> 32.1 us
  blocking collectives: 23.5 us -> 0 us
  local copies, waits for them, and re-layouts: 1.71 us -> 6.56 us
  waiting for transfers between devices: 71.5 us -> 67.1 us
    ppermute x0 -> x15, starting transfers between devices: none -> 32 us  [the longest x7 31.5 us: dense_block(): lax.ppermute(going_down, 'node', [(d, (d - 1) % ways) for d in range(ways)])]
    all_gather x1 -> x0, blocking collectives: 23.5 us -> none  [dense_block(): every_share = lax.all_gather(dense_shares, 'node', axis=0, tiled=True)]
    all_gather x1, waiting for transfers between devices: 15.2 us -> 0.02 us  [dense_block(): every_row = lax.all_gather(normed, 'node', axis=0, tiled=True)]
    ppermute x0 -> x15, waiting for transfers between devices: none -> 10.6 us  [the longest x8 10.2 us: dense_block(): lax.ppermute(going_up, 'node', [(d, (d + 1) % ways) for d in range(ways)])]
    dynamic_update_slice x0 -> x16, local copies, waits for them, and re-layouts: none -> 3.91 us  [the longest x7 1.9 us: dense_block(): lax.dynamic_update_slice_in_dim(every_share, going_down, (here + far) % w...]
  transfers between devices with their start and end apart: 2 -> 17, of which waited for: 2 -> 12; matrix products, arithmetic and copies ran while one was open for 5% -> 8% of each run, Pallas kernels for 0% -> 0%
where the time goes in v1:
time: 140 us; the launch traced here: 139 us
  waiting for transfers between devices  67.1 us (48%)
  starting transfers between devices  32.1 us (23%)
  between operations  14.2 us (10%)
  matrix products  13.3 us (10%)
  local copies, waits for them, and re-layouts  6.56 us (5%)
  other arithmetic  6.06 us (4%)
    reduce_scatter x1, waiting for transfers between devices, dense_block(): total = lax.psum_scatter(summed, 'node', scatter_dimension=0, tiled=True)  56.4 us
    ppermute x7, starting transfers between devices, dense_block(): lax.ppermute(going_down, 'node', [(d, (d - 1) % ways) for d in range(ways)])  31.5 us
    ppermute x8, waiting for transfers between devices, dense_block(): lax.ppermute(going_up, 'node', [(d, (d + 1) % ways) for d in range(ways)])  10.2 us
    dot_general x1, matrix products, dense_block(): jnp.dot(inner, w_down[expert], preferred_element_type=jnp.float32)  5.91 us
    dot_general x1, matrix products, dense_block(): jnp.dot(every_row, w_gate[expert], preferred_element_type=jnp.float32)  4.08 us
  transfers between devices with their start and end apart: 17, of which 12 were waited for; matrix products, arithmetic and copies ran while one was open for 8% of the time, Pallas kernels for 0%

profile of v1, /device:TPU:0, one launch (start us, length us, event | category | flops | bytes accessed | tf_op | source)
XLA Modules:
  0.0 139.4 jit_solution(14283752486971126922)
XLA Ops:
  7.2 1.1 fusion.37
  8.4 1.6 %fusion.39 = bf16[16,2048]{1,0:T(8,128)(2,1)} fusion(bf16[16,2048]{1,0:T(8,128)(2,1)} %param.13, f32[2048]{0:T(1024)} %param.14, f32[16]{0:T(128)S(1)} %add_sqrt_fusion), kind=kLoop, calls=%fused_computation.30 | loop fusion | flops 131072 | bytes 139328 | tf_op jit(solution)/shard_map/convert_element_type | solution.py:164
  10.0 0.7 reduce_sum.36
  10.7 0.7 broadcast_divide_fusion
  11.4 0.1 copy.24
  11.5 0.8 copy.23
  12.2 0.1 select_reduce_fusion
  12.3 0.5 collective-permute-start
  12.8 5.1 %collective-permute-start.1 = (f32[16,16]{1,0:T(8,128)S(1)}, f32[16,16]{1,0:T(8,128)S(1)}, u32[]{:S(2)}, u32[]{:S(2)}) collective-permute-start(f32[16,16]{1,0:T(8,128)S(1)} %select_reduce_fusion), channel_id=1, source_target_pairs={{0,15},{1,0},{2,1},{3,2},{4,3},{5,4},{6,5},{7,6},{8,7},{9,8},{10,9... | collective-permute-start | bytes 3080 | tf_op jit(solution)/shard_map/ppermute | solution.py:83
  17.9 0.1 copy.25
  18.0 1.2 collective-permute-done
  19.2 0.1 collective-permute-done.1
  19.3 4.4 %collective-permute-start.3 = (f32[16,16]{1,0:T(8,128)S(1)}, f32[16,16]{1,0:T(8,128)S(1)}, u32[]{:S(2)}, u32[]{:S(2)}) collective-permute-start(f32[16,16]{1,0:T(8,128)S(1)} %collective-permute-done.1), channel_id=1, source_target_pairs={{0,15},{1,0},{2,1},{3,2},{4,3},{5,4},{6,5},{7,6},{8,7},{9,8},{10,9... | collective-permute-start | bytes 3080 | tf_op jit(solution)/shard_map/ppermute | solution.py:83
  23.7 1.3 collective-permute-done.2
  25.0 0.1 collective-permute-done.3
  25.0 4.4 %collective-permute-start.5 = (f32[16,16]{1,0:T(8,128)S(1)}, f32[16,16]{1,0:T(8,128)S(1)}, u32[]{:S(2)}, u32[]{:S(2)}) collective-permute-start(f32[16,16]{1,0:T(8,128)S(1)} %collective-permute-done.3), channel_id=1, source_target_pairs={{0,15},{1,0},{2,1},{3,2},{4,3},{5,4},{6,5},{7,6},{8,7},{9,8},{10,9... | collective-permute-start | bytes 3080 | tf_op jit(solution)/shard_map/ppermute | solution.py:83
  29.5 1.3 collective-permute-done.4
  30.7 0.1 collective-permute-done.5
  30.8 4.5 %collective-permute-start.7 = (f32[16,16]{1,0:T(8,128)S(1)}, f32[16,16]{1,0:T(8,128)S(1)}, u32[]{:S(2)}, u32[]{:S(2)}) collective-permute-start(f32[16,16]{1,0:T(8,128)S(1)} %collective-permute-done.5), channel_id=1, source_target_pairs={{0,15},{1,0},{2,1},{3,2},{4,3},{5,4},{6,5},{7,6},{8,7},{9,8},{10,9... | collective-permute-start | bytes 3080 | tf_op jit(solution)/shard_map/ppermute | solution.py:83
  35.3 1.2 collective-permute-done.6
  36.5 0.1 collective-permute-done.7
  36.7 4.4 %collective-permute-start.9 = (f32[16,16]{1,0:T(8,128)S(1)}, f32[16,16]{1,0:T(8,128)S(1)}, u32[]{:S(2)}, u32[]{:S(2)}) collective-permute-start(f32[16,16]{1,0:T(8,128)S(1)} %collective-permute-done.7), channel_id=1, source_target_pairs={{0,15},{1,0},{2,1},{3,2},{4,3},{5,4},{6,5},{7,6},{8,7},{9,8},{10,9... | collective-permute-start | bytes 3080 | tf_op jit(solution)/shard_map/ppermute | solution.py:83
  41.1 1.3 collective-permute-done.8
  42.4 4.4 %collective-permute-start.11 = (f32[16,16]{1,0:T(8,128)S(1)}, f32[16,16]{1,0:T(8,128)S(1)}, u32[]{:S(2)}, u32[]{:S(2)}) collective-permute-start(f32[16,16]{1,0:T(8,128)S(1)} %collective-permute-done.9), channel_id=1, source_target_pairs={{0,15},{1,0},{2,1},{3,2},{4,3},{5,4},{6,5},{7,6},{8,7},{9,8},{10,9... | collective-permute-start | bytes 3080 | tf_op jit(solution)/shard_map/ppermute | solution.py:83
  46.8 1.3 collective-permute-done.10
  48.2 0.3 dynamic_update_slice.48
  48.4 0.1 copy.26
  48.5 0.2 dynamic_update_slice.49
  48.8 0.3 dynamic_update_slice.50
  49.1 0.2 dynamic_update_slice.51
  49.4 0.1 copy.29
  49.4 0.3 dynamic_update_slice.52
  49.7 4.4 %collective-permute-start.13 = (f32[16,16]{1,0:T(8,128)S(1)}, f32[16,16]{1,0:T(8,128)S(1)}, u32[]{:S(2)}, u32[]{:S(2)}) collective-permute-start(f32[16,16]{1,0:T(8,128)S(1)} %collective-permute-done.11), channel_id=1, source_target_pairs={{0,15},{1,0},{2,1},{3,2},{4,3},{5,4},{6,5},{7,6},{8,7},{9,8},{10,9... | collective-permute-start | bytes 3080 | tf_op jit(solution)/shard_map/ppermute | solution.py:83
  54.1 0.1 copy.30
  54.2 0.3 dynamic_update_slice.53
  54.5 0.1 copy.31
  54.5 0.3 dynamic_update_slice.54
  54.8 0.1 copy.32
  54.9 0.2 dynamic_update_slice.55
  55.2 0.3 dynamic_update_slice.56
  55.5 0.2 dynamic_update_slice.57
  55.7 0.1 copy.35
  55.8 0.3 dynamic_update_slice.58
  56.1 0.1 copy.36
  56.1 0.2 dynamic_update_slice.59
  56.4 0.1 copy.37
  56.4 0.3 dynamic_update_slice.60
  56.7 0.1 copy.38
  56.8 0.2 dynamic_update_slice.61
  57.0 0.1 copy.39
  57.1 0.3 dynamic_update_slice.62
  57.4 2.6 %collective-permute-done.14 = f32[16,16]{1,0:T(8,128)S(1)} collective-permute-done((f32[16,16]{1,0:T(8,128)S(1)}, f32[16,16]{1,0:T(8,128)S(1)}, u32[]{:S(2)}, u32[]{:S(2)}) %collective-permute-start.14) | collective-permute-done | bytes 1056 | tf_op jit(solution)/shard_map/ppermute | solution.py:78
  59.9 0.1 copy.40
  60.0 0.1 dynamic_update_slice.63
  60.2 4.1 %fusion.4 = f32[256,768]{1,0:T(8,128)} fusion(bf16[256,2048]{1,0:T(8,128)(2,1)} %all-gather.2.cloned.1.call-done, bf16[1,2048,768]{2,1,0:T(8,128)(2,1)} %param.17), kind=kOutput, calls=%fused_computation.4 | convolution fusion | flops 805306368 | bytes 4980736 | tf_op jit(solution)/shard_map/dot_general | solution.py:94
  64.3 5.9 %multiply_select_fusion = f32[256,2048]{1,0:T(8,128)} fusion(f32[256]{0:T(256)S(1)} %bitcast.65, pred[256]{0:T(512)(128)(4,1)S(1)} %get-tuple-element.2, bf16[1,768,2048]{2,1,0:T(8,128)(2,1)S(1)} %copy-done, bf16[256,2048]{1,0:T(8,128)(2,1)} %all-gather.2.cloned.1.call-done, bf16[1,2048,768]{2,1,0:T(8,128)(2,1)} %param.18, f32[256,768]{1,0:T(8,128)} %fusion.4), kind=kOutput, calls=%fused_computation.8 | convolution fusion | flops 1613889536 | bytes 10224896 | tf_op jit(solution)/shard_map/dot_general | solution.py:97
  70.3 0.1 iota_compare_fusion.1
  70.3 0.1 fusion.45
  70.5 1.7 %fusion.54 = (f32[4,4,8]{2,1,0:T(4,128)S(1)}, f32[4,4,8,256]{3,2,1,0:T(8,128)S(1)}) fusion(bf16[1,4,32,128]{3,1,2,0:T(4,128)(2,1)S(1)} %bitcast.61, pred[4,256]{1,0:T(4,128)(4,1)S(1)} %iota_compare_fusion.1, bf16[4,256,512]{2,1,0:T(8,128)(2,1)} %param.21), kind=kOutput, calls=%fused_computation.58 | convolution fusion | flops 8486784 | bytes 1213952 | tf_op jit(solution)/shard_map/rkgd,rlkd->rkgl/dot_general | solution.py:116
  72.2 0.2 fusion.40
  72.4 1.5 %fusion.20 = bf16[1,4,32,128]{3,2,1,0:T(8,128)(2,1)S(1)} fusion(f32[4,4,8,256]{3,2,1,0:T(8,128)S(1)} %get-tuple-element.7, f32[4,4,8]{2,1,0:T(4,128)S(1)} %get-tuple-element.5, f32[4,4,8]{2,1,0:T(4,128)S(1)} %multiply_maximum_fusion, pred[4,256]{1,0:T(4,128)(4,1)S(1)} %iota_compare_fusion.1, f32[4,4,128]{2,1,0:T(4,128)S(1)} %reshape.64, ...), kind=kOutput, calls=%fused_computation.15 | convolution fusion | flops 8568832 | bytes 1223168 | tf_op jit(solution)/shard_map/rkgl,rlkd->rkgd/dot_general | solution.py:138
  73.9 0.6 copy.70
  74.6 56.4 %reduce-scatter.2.cloned.1.call-done = f32[16,2048]{1,0:T(8,128)} async-done(((f32[256,2048]{1,0:T(8,128)}), f32[16,2048]{1,0:T(8,128)}) %reduce-scatter.2.cloned.1.call-update) | async-done | bytes 131088 | tf_op jit(solution)/shard_map/reduce_scatter | solution.py:103
  131.0 1.5 %convert_element_type.49 = bf16[16,2048]{1,0:T(8,128)(2,1)} convert(f32[16,2048]{1,0:T(8,128)} %reduce-scatter.2.cloned.1.call-done) | non-fusion elementwise | flops 32768 | bytes 196608 | tf_op jit(solution)/shard_map/convert_element_type | solution.py:104
  (37 shorter events, 0.6 us)
Async XLA Ops:
  7.2 57.1 %copy-start = (bf16[1,768,2048]{2,1,0:T(8,128)(2,1)S(1)}, bf16[1,768,2048]{2,1,0:T(8,128)(2,1)}, u32[]{:S(2)}) copy-start(bf16[1,768,2048]{2,1,0:T(8,128)(2,1)} %param.19) | copy-start | bytes 9437188
  7.2 53.0 %all-gather.2.cloned.1.call-start = ((), (), s32[]{:S(2)}) async-start(), calls=%async_computation.1 | async-start | bytes 1114112 | tf_op jit(solution)/shard_map/all_gather | solution.py:70
  9.9 121.1 %reduce-scatter.2.cloned.1.call-start = ((), (), s32[]{:S(2)}) async-start(), calls=%async_computation.2 | async-start | bytes 2228224 | tf_op jit(solution)/shard_map/reduce_scatter | solution.py:103
  12.3 6.8 %collective-permute-start = (f32[16,16]{1,0:T(8,128)S(1)}, f32[16,16]{1,0:T(8,128)S(1)}, u32[]{:S(2)}, u32[]{:S(2)}) collective-permute-start(f32[16,16]{1,0:T(8,128)S(1)} %select_reduce_fusion), channel_id=1, source_target_pairs={{0,1},{1,2},{2,3},{3,4},{4,5},{5,6},{6,7},{7,8},{8,9},{9,10},{10,1... | collective-permute-start | bytes 3080 | tf_op jit(solution)/shard_map/ppermute | solution.py:78
  12.8 6.4 %collective-permute-start.1 = (f32[16,16]{1,0:T(8,128)S(1)}, f32[16,16]{1,0:T(8,128)S(1)}, u32[]{:S(2)}, u32[]{:S(2)}) collective-permute-start(f32[16,16]{1,0:T(8,128)S(1)} %select_reduce_fusion), channel_id=1, source_target_pairs={{0,15},{1,0},{2,1},{3,2},{4,3},{5,4},{6,5},{7,6},{8,7},{9,8},{10,9... | collective-permute-start | bytes 3080 | tf_op jit(solution)/shard_map/ppermute | solution.py:83
  19.2 5.8 %collective-permute-start.2 = (f32[16,16]{1,0:T(8,128)S(1)}, f32[16,16]{1,0:T(8,128)S(1)}, u32[]{:S(2)}, u32[]{:S(2)}) collective-permute-start(f32[16,16]{1,0:T(8,128)S(1)} %collective-permute-done), channel_id=1, source_target_pairs={{0,1},{1,2},{2,3},{3,4},{4,5},{5,6},{6,7},{7,8},{8,9},{9,10},{10,1... | collective-permute-start | bytes 3080 | tf_op jit(solution)/shard_map/ppermute | solution.py:78
  19.3 5.8 %collective-permute-start.3 = (f32[16,16]{1,0:T(8,128)S(1)}, f32[16,16]{1,0:T(8,128)S(1)}, u32[]{:S(2)}, u32[]{:S(2)}) collective-permute-start(f32[16,16]{1,0:T(8,128)S(1)} %collective-permute-done.1), channel_id=1, source_target_pairs={{0,15},{1,0},{2,1},{3,2},{4,3},{5,4},{6,5},{7,6},{8,7},{9,8},{10,9... | collective-permute-start | bytes 3080 | tf_op jit(solution)/shard_map/ppermute | solution.py:83
  25.0 5.8 %collective-permute-start.4 = (f32[16,16]{1,0:T(8,128)S(1)}, f32[16,16]{1,0:T(8,128)S(1)}, u32[]{:S(2)}, u32[]{:S(2)}) collective-permute-start(f32[16,16]{1,0:T(8,128)S(1)} %collective-permute-done.2), channel_id=1, source_target_pairs={{0,1},{1,2},{2,3},{3,4},{4,5},{5,6},{6,7},{7,8},{8,9},{9,10},{10,1... | collective-permute-start | bytes 3080 | tf_op jit(solution)/shard_map/ppermute | solution.py:78
  25.0 5.8 %collective-permute-start.5 = (f32[16,16]{1,0:T(8,128)S(1)}, f32[16,16]{1,0:T(8,128)S(1)}, u32[]{:S(2)}, u32[]{:S(2)}) collective-permute-start(f32[16,16]{1,0:T(8,128)S(1)} %collective-permute-done.3), channel_id=1, source_target_pairs={{0,15},{1,0},{2,1},{3,2},{4,3},{5,4},{6,5},{7,6},{8,7},{9,8},{10,9... | collective-permute-start | bytes 3080 | tf_op jit(solution)/shard_map/ppermute | solution.py:83
  30.7 5.8 %collective-permute-start.6 = (f32[16,16]{1,0:T(8,128)S(1)}, f32[16,16]{1,0:T(8,128)S(1)}, u32[]{:S(2)}, u32[]{:S(2)}) collective-permute-start(f32[16,16]{1,0:T(8,128)S(1)} %collective-permute-done.4), channel_id=1, source_target_pairs={{0,1},{1,2},{2,3},{3,4},{4,5},{5,6},{6,7},{7,8},{8,9},{9,10},{10,1... | collective-permute-start | bytes 3080 | tf_op jit(solution)/shard_map/ppermute | solution.py:78
  30.8 5.8 %collective-permute-start.7 = (f32[16,16]{1,0:T(8,128)S(1)}, f32[16,16]{1,0:T(8,128)S(1)}, u32[]{:S(2)}, u32[]{:S(2)}) collective-permute-start(f32[16,16]{1,0:T(8,128)S(1)} %collective-permute-done.5), channel_id=1, source_target_pairs={{0,15},{1,0},{2,1},{3,2},{4,3},{5,4},{6,5},{7,6},{8,7},{9,8},{10,9... | collective-permute-start | bytes 3080 | tf_op jit(solution)/shard_map/ppermute | solution.py:83
  36.5 5.9 %collective-permute-start.8 = (f32[16,16]{1,0:T(8,128)S(1)}, f32[16,16]{1,0:T(8,128)S(1)}, u32[]{:S(2)}, u32[]{:S(2)}) collective-permute-start(f32[16,16]{1,0:T(8,128)S(1)} %collective-permute-done.6), channel_id=1, source_target_pairs={{0,1},{1,2},{2,3},{3,4},{4,5},{5,6},{6,7},{7,8},{8,9},{9,10},{10,1... | collective-permute-start | bytes 3080 | tf_op jit(solution)/shard_map/ppermute | solution.py:78
  36.7 5.8 %collective-permute-start.9 = (f32[16,16]{1,0:T(8,128)S(1)}, f32[16,16]{1,0:T(8,128)S(1)}, u32[]{:S(2)}, u32[]{:S(2)}) collective-permute-start(f32[16,16]{1,0:T(8,128)S(1)} %collective-permute-done.7), channel_id=1, source_target_pairs={{0,15},{1,0},{2,1},{3,2},{4,3},{5,4},{6,5},{7,6},{8,7},{9,8},{10,9... | collective-permute-start | bytes 3080 | tf_op jit(solution)/shard_map/ppermute | solution.py:83
  42.4 5.8 %collective-permute-start.10 = (f32[16,16]{1,0:T(8,128)S(1)}, f32[16,16]{1,0:T(8,128)S(1)}, u32[]{:S(2)}, u32[]{:S(2)}) collective-permute-start(f32[16,16]{1,0:T(8,128)S(1)} %collective-permute-done.8), channel_id=1, source_target_pairs={{0,1},{1,2},{2,3},{3,4},{4,5},{5,6},{6,7},{7,8},{8,9},{9,10},{10,1... | collective-permute-start | bytes 3080 | tf_op jit(solution)/shard_map/ppermute | solution.py:78
  42.4 7.3 %collective-permute-start.11 = (f32[16,16]{1,0:T(8,128)S(1)}, f32[16,16]{1,0:T(8,128)S(1)}, u32[]{:S(2)}, u32[]{:S(2)}) collective-permute-start(f32[16,16]{1,0:T(8,128)S(1)} %collective-permute-done.9), channel_id=1, source_target_pairs={{0,15},{1,0},{2,1},{3,2},{4,3},{5,4},{6,5},{7,6},{8,7},{9,8},{10,9... | collective-permute-start | bytes 3080 | tf_op jit(solution)/shard_map/ppermute | solution.py:83
  48.2 6.0 %collective-permute-start.12 = (f32[16,16]{1,0:T(8,128)S(1)}, f32[16,16]{1,0:T(8,128)S(1)}, u32[]{:S(2)}, u32[]{:S(2)}) collective-permute-start(f32[16,16]{1,0:T(8,128)S(1)} %collective-permute-done.10), channel_id=1, source_target_pairs={{0,1},{1,2},{2,3},{3,4},{4,5},{5,6},{6,7},{7,8},{8,9},{9,10},{10,1... | collective-permute-start | bytes 3080 | tf_op jit(solution)/shard_map/ppermute | solution.py:78
  49.7 7.3 %collective-permute-start.13 = (f32[16,16]{1,0:T(8,128)S(1)}, f32[16,16]{1,0:T(8,128)S(1)}, u32[]{:S(2)}, u32[]{:S(2)}) collective-permute-start(f32[16,16]{1,0:T(8,128)S(1)} %collective-permute-done.11), channel_id=1, source_target_pairs={{0,15},{1,0},{2,1},{3,2},{4,3},{5,4},{6,5},{7,6},{8,7},{9,8},{10,9... | collective-permute-start | bytes 3080 | tf_op jit(solution)/shard_map/ppermute | solution.py:83
  54.2 5.8 %collective-permute-start.14 = (f32[16,16]{1,0:T(8,128)S(1)}, f32[16,16]{1,0:T(8,128)S(1)}, u32[]{:S(2)}, u32[]{:S(2)}) collective-permute-start(f32[16,16]{1,0:T(8,128)S(1)} %collective-permute-done.12), channel_id=1, source_target_pairs={{0,1},{1,2},{2,3},{3,4},{4,5},{5,6},{6,7},{7,8},{8,9},{9,10},{10,1... | collective-permute-start | bytes 3080 | tf_op jit(solution)/shard_map/ppermute | solution.py:78
  64.2 6.0 %copy-start.2 = (bf16[4,512]{1,0:T(4,128)(2,1)S(1)}, bf16[4,512]{1,0:T(4,128)(2,1)}, u32[]{:S(2)}) copy-start(bf16[4,512]{1,0:T(4,128)(2,1)} %param.23) | copy-start | bytes 12292
  64.3 6.0 %copy-start.3 = (bf16[4,512]{1,0:T(4,128)(2,1)S(1)}, bf16[4,512]{1,0:T(4,128)(2,1)}, u32[]{:S(2)}) copy-start(bf16[4,512]{1,0:T(4,128)(2,1)} %param.24) | copy-start | bytes 12292
  64.3 6.0 %copy-start.4 = (s32[4]{0:T(128)S(1)}, s32[4]{0:T(128)}, u32[]{:S(2)}) copy-start(s32[4]{0:T(128)} %param.25) | copy-start | bytes 52
  64.3 6.1 %copy-start.1 = (bf16[4,4096]{1,0:T(4,128)(2,1)S(1)}, bf16[4,4096]{1,0:T(4,128)(2,1)}, u32[]{:S(2)}) copy-start(bf16[4,4096]{1,0:T(4,128)(2,1)} %param.20) | copy-start | bytes 98308
Sparse Core Ops, SparseCore 0:
  10.7 40.7 all-gather.1
  70.3 60.6 reduce-scatter.1
